TPU v7x, 32 devices: a whole 2x2x4 slice. The times are simulated.
32 devices in a mesh: blk: 16 (over z, y, x), band: 2 (over core).
Axes of the slice: x: 2, y: 2, z: 4, core: 2. Of those that a mesh axis runs over, the one named last changes fastest.
Arguments:
- traces: bfloat16 [1024, 2, 8192], P('blk', None, 'band'), may hold values from -80 to 80
- sources: bfloat16 [32, 2, 8192], P('blk', None, 'band'), may hold values from -80 to 80
- owner: int32 [1024, 1], P('blk'), may hold values from 0 to 15; in each aligned block of 64 rows (0 to 63, 64 to 127, ...) at most 8 rows name the same one
Outputs:
- gathers: float32 [32, 4, 128, 256], P('blk', None, 'band')
Inputs may be any that keep to these rules, and one draw needn't show every extreme that they name: Among the 64 stations of one device's rows, at most 8 name the same owner block, and some owner block is named by exactly 8 of them in every draw.
All inputs are finite; a program needn't handle non-finite values.
Results may differ from a plain program's by a relative error of at most 0.017.
Values may be sent and summed in bfloat16 or wider, within the bound.
No kernel may reach another device: no remote copies, remote signals or barrier semaphores. Data moves between devices by JAX's collectives and lax.ppermute only.
A program may use at most 128 MiB of HBM per device.

v0:
```python
import math
import jax
import jax.numpy as jnp
from jax import lax
from jax.sharding import PartitionSpec as P

BINS = 8192
LAGS = 2048
DEC = 8
PERIOD = BINS // DEC
EPS = 1e-06


def per_device(traces, sources, owner):
    blocks = lax.axis_size("blk")
    station_count = traces.shape[0]
    source_count = sources.shape[0]
    group_bins = traces.shape[2]
    folds = group_bins // PERIOD
    capacity = max(2, 2 * station_count // blocks)
    lags_out = LAGS // DEC
    offsets = blocks // 4
    all_sources = lax.all_gather(sources, "blk", axis=0, tiled=True)
    trace_float = traces.astype(jnp.float32)
    all_source_float = all_sources.astype(jnp.float32)
    trace_power, source_power = lax.psum(
        (
            jnp.sum(trace_float * trace_float, axis=(1, 2)),
            jnp.sum(all_source_float * all_source_float, axis=(1, 2)),
        ),
        "band",
    )
    white_traces = (
        (trace_float * lax.rsqrt(trace_power / (2 * BINS) + EPS)[:, None, None])
        .astype(jnp.bfloat16)
        .reshape(station_count, 2 * group_bins)
    )
    white_sources = (
        (all_source_float * lax.rsqrt(source_power / (2 * BINS) + EPS)[:, None, None])
        .astype(jnp.bfloat16)
        .astype(jnp.float32)
        .reshape(blocks, source_count, 2, folds, PERIOD)
    )
    owners = owner[:, 0]
    owner_hits = (owners[:, None] == jnp.arange(blocks, dtype=jnp.int32)[None, :]).astype(jnp.int32)
    earlier = jnp.cumsum(owner_hits, axis=0) - owner_hits
    arrival = jnp.sum(owner_hits * earlier, axis=1)
    slot_index = owners * capacity + arrival
    placing = (
        jnp.arange(blocks * capacity, dtype=jnp.int32)[:, None] == slot_index[None, :]
    ).astype(jnp.bfloat16)
    placed = jnp.dot(placing, white_traces, preferred_element_type=jnp.float32)
    placed = placed.reshape(blocks, capacity, 2, folds, PERIOD)
    bin_index = jnp.arange(PERIOD, dtype=jnp.int32)
    lag_value = (jnp.arange(lags_out, dtype=jnp.int32) - lags_out // 2) * DEC
    phase_angle = jnp.mod(bin_index[:, None] * lag_value[None, :], BINS).astype(jnp.float32) * (
        2.0 * math.pi / BINS
    )
    table = jnp.concatenate([jnp.cos(phase_angle), jnp.sin(phase_angle)], axis=0).astype(
        jnp.bfloat16
    )
    norm_scale = BINS ** (-0.5)
    real_s = white_sources[:, None, :, 0]
    imag_s = white_sources[:, None, :, 1]
    cross = []
    for offset in range(offsets):
        visiting = jnp.roll(placed, offset, axis=0)
        real_t = visiting[:, :, None, 0]
        imag_t = visiting[:, :, None, 1]
        even = jnp.sum(real_t * real_s + imag_t * imag_s, axis=3)
        odd = jnp.sum(real_t * imag_s - imag_t * real_s, axis=3)
        cross.append(jnp.concatenate([even, odd], axis=-1))
    cross = jnp.stack(cross, axis=1).astype(jnp.bfloat16)
    rows = blocks * offsets * capacity * source_count
    partial = jnp.dot(cross.reshape(rows, 2 * PERIOD), table, preferred_element_type=jnp.float32)
    partial = (partial * norm_scale).astype(jnp.bfloat16)
    partial = partial.reshape(blocks, offsets, capacity, source_count, lags_out)
    arrived = lax.all_to_all(partial, "blk", split_axis=0, concat_axis=0, tiled=True)
    summed = lax.psum_scatter(arrived.astype(jnp.float32), "band", scatter_dimension=0, tiled=True)
    half = summed.shape[0]
    return jnp.transpose(summed, (3, 1, 0, 2, 4)).reshape(
        source_count, offsets, half * capacity, lags_out
    )


def solution(mesh):
    placed = (P("blk", None, "band"), P("blk", None, "band"), P("blk", None))
    return jax.shard_map(
        per_device,
        mesh=mesh,
        in_specs=placed,
        out_specs=P("blk", None, "band", None),
        check_vma=False,
    )
```

profile of v0, /device:TPU:0, one launch (start us, length us, event | category | flops | bytes accessed | tf_op | source)
XLA Modules:
  0.0 150.7 jit_solution(14130566093052021480)
XLA Ops:
  6.5 0.0 reduce-scatter.2.cloned.1.call-start
  6.5 45.7 %all_gather.3 = bf16[32,2,4096]{2,1,0:T(2,128)(2,1)S(1)} all-gather(bf16[2,2,4096]{2,1,0:T(2,128)(2,1)} %param.4), channel_id=1, replica_groups=mesh['blk'=16,'band'=2] {'blk'}, dimensions={0}, use_global_device_ids=true | all-gather | bytes 557056 | tf_op jit(solution)/shard_map/all_gather | solution.py:23
  52.2 0.8 copy-done.4
  53.0 0.8 fusion.12
  53.8 2.8 %fusion = f32[64]{0:T(128)S(1)} fusion(bf16[64,2,4096]{2,1,0:T(2,128)(2,1)} %param.3), kind=kLoop, calls=%fused_computation.17 | loop fusion | flops 1572800 | bytes 1048832 | tf_op jit(solution)/shard_map/reduce_sum | solution.py:28
  56.6 2.5 %all-reduce = (f32[32]{0:T(128)S(1)}, f32[64]{0:T(128)S(1)}) all-reduce(f32[32]{0:T(128)S(1)} %fusion.12, f32[64]{0:T(128)S(1)} %fusion), channel_id=1, replica_groups=mesh['blk'=16,'band'=2] {'band'}, use_global_device_ids=true, to_apply=%region_5.6 | all-reduce | flops 96 | bytes 768 | tf_op jit(solution)/shard_map/psum | solution.py:26
  59.1 2.5 %fusion.1 = bf16[64,2,4096]{2,1,0:T(2,128)(2,1)S(1)} fusion(bf16[64,2,4096]{2,1,0:T(2,128)(2,1)} %param.3, f32[64]{0:T(128)S(1)} %add_rsqrt_fusion.1), kind=kLoop, calls=%fused_computation.18 | loop fusion | flops 1572864 | bytes 2097408 | tf_op jit(solution)/shard_map/convert_element_type | solution.py:35
  61.6 0.6 copy.44
  62.2 0.0 copy-done.8
  62.2 0.1 fusion.26
  62.3 0.1 reduce_window_sum.11
  62.4 0.2 select_reduce_fusion
  62.6 0.7 fusion.24
  63.3 0.2 slice.107
  63.5 0.9 slice.106
  64.5 2.1 %slice.103 = f32[112,8192]{1,0:T(8,128)} slice(f32[128,8192]{1,0:T(8,128)S(1)} %fusion.24), slice={[0:112], [0:8192]} | slice | bytes 7340032 | tf_op jit(solution)/shard_map/jit(_roll_static)/slice | solution.py:67
  66.6 0.8 slice.102
  67.4 2.1 %slice.99 = f32[120,8192]{1,0:T(8,128)} slice(f32[128,8192]{1,0:T(8,128)S(1)} %fusion.24), slice={[0:120], [0:8192]} | slice | bytes 7864320 | tf_op jit(solution)/shard_map/jit(_roll_static)/slice | solution.py:67
  69.6 0.7 slice.98
  70.3 2.4 %slice_bitcast_fusion.1 = (f32[16,8,4,1024]{3,1,2,0:T(8,128)}, f32[16,8,4,1024]{3,1,2,0:T(8,128)}) fusion(f32[16,8,2,4,1024]{4,1,3,2,0:T(8,128)S(1)} %bitcast.46), kind=kLoop, calls=%fused_computation.32 | loop fusion | bytes 8388608 | tf_op jit(solution)/shard_map/mul | solution.py:70
  72.7 0.0 copy-done.5
  72.7 1.5 %fusion.23 = f32[32,2,4096]{2,1,0:T(2,128)} fusion(f32[32]{0:T(128)S(1)} %add_rsqrt_fusion, bf16[32,2,4096]{2,1,0:T(2,128)(2,1)S(1)} %copy-done.5), kind=kLoop, calls=%fused_computation.57 | loop fusion | flops 1048576 | bytes 1572992 | tf_op jit(solution)/shard_map/reshape | solution.py:42
  74.2 3.3 %reshape.51 = f32[16,2,2,4,1024]{4,3,2,1,0:T(4,128)} reshape(f32[32,2,4096]{2,1,0:T(2,128)} %fusion.23) | data formatting | bytes 2097152 | tf_op jit(solution)/shard_map/reshape | solution.py:42
  77.6 1.3 slice_bitcast_fusion.3
  78.9 1.6 %fusion.3 = (f32[16,8,4,1024]{3,1,2,0:T(8,128)S(1)}, f32[16,8,4,1024]{3,1,2,0:T(8,128)S(1)}) fusion(f32[3,8,2,4,1024]{4,1,3,2,0:T(8,128)} %bitcast.52, f32[13,8,2,4,1024]{4,1,3,2,0:T(8,128)S(1)} %bitcast.49), kind=kLoop, calls=%fused_computation.20 | loop fusion | flops 1048576 | bytes 8388608 | tf_op jit(solution)/shard_map/mul | solution.py:70
  80.5 0.6 copy-done.1
  81.2 0.1 copy-done.6
  81.3 0.5 fusion.5
  81.8 1.6 %copy-done = f32[120,8192]{1,0:T(8,128)S(1)} copy-done((f32[120,8192]{1,0:T(8,128)S(1)}, f32[120,8192]{1,0:T(8,128)}, u32[]{:S(2)}) %copy-start) | copy-done | bytes 3932184
  83.4 0.0 copy-done.7
  83.4 0.5 fusion.7
  83.9 1.1 copy-done.2
  85.0 0.6 copy-done.3
  85.6 7.3 %add_reduce_fusion.3 = (bf16[16,8,2,1024]{3,1,2,0:T(8,128)(2,1)S(1)}, bf16[16,8,2,1024]{3,1,2,0:T(8,128)(2,1)S(1)}, bf16[16,8,2,1024]{3,1,2,0:T(8,128)(2,1)S(1)}...) fusion(f32[16,2,4,1024]{3,2,1,0:T(4,128)S(1)} %get-tuple-elemen, ...), kind=kLoop, calls=%fused_computation.14 | loop fusion | flops 31457280 | bytes 22020096 | tf_op jit(solution)/shard_map/reduce_sum | solution.py:70
  92.9 0.2 maximum_bitcast_fusion
  93.1 0.2 maximum_bitcast_fusion.2
  93.3 0.6 pad_maximum_fusion
  93.9 6.3 %copy.41 = bf16[16,4,8,2,2048]{4,3,2,1,0:T(2,128)(2,1)} copy(bf16[16,4,8,2,2048]{4,2,3,0,1:T(8,128)(2,1)S(1)} %pad_maximum_fusion) | data formatting | bytes 8388608 | tf_op jit(solution)/shard_map/stack | solution.py:73
  100.2 7.2 %convert_element_type.39 = bf16[1024,2048]{1,0:T(8,128)(2,1)} reshape(bf16[16,4,8,2,2048]{4,3,2,1,0:T(2,128)(2,1)} %copy.41) | data formatting | bytes 8388608 | tf_op jit(solution)/shard_map/convert_element_type | solution.py:73
  107.4 4.4 %cosine_convert_fusion = (bf16[1024,256]{1,0:T(8,128)(2,1)S(1)}, bf16[1024,256]{1,0:T(8,128)(2,1)S(1)}) fusion(s32[256]{0:T(256)S(1)} %add_multiply_fusion), kind=kLoop, calls=%fused_computation.53 | loop fusion | flops 4194304 | bytes 1049600 | tf_op jit(solution)/shard_map/convert.1
  111.8 3.4 %fusion.11 = bf16[1024,256]{1,0:T(8,128)(2,1)S(1)} fusion(bf16[1024,2048]{1,0:T(8,128)(2,1)} %convert_element_type.39, bf16[1024,256]{1,0:T(8,128)(2,1)S(1)} %get-tuple-element.32, bf16[1024,256]{1,0:T(8,128)(2,1)S(1)} %get-tuple-element.31), kind=kOutput, calls=%fused_computation.39 | convolution fusion | flops 1076363264 | bytes 5767168 | tf_op jit(solution)/shard_map/dot_general | solution.py:75
  115.2 0.2 reshape.48
  115.4 0.1 copy.42
  115.5 18.1 %all_to_all.5 = bf16[16,4,8,2,256]{4,2,3,1,0:T(8,128)(2,1)S(1)} all-to-all(bf16[16,4,8,2,256]{4,2,3,1,0:T(8,128)(2,1)S(1)} %copy.42), channel_id=1, replica_groups=mesh['blk'=16,'band'=2] {'blk'}, dimensions={0} | all-to-all | bytes 1048576 | tf_op jit(solution)/shard_map/all_to_all | solution.py:78
  133.6 1.1 convert_element_type.42
  134.7 0.0 reduce-scatter.2.cloned.1.call-update
  134.8 7.2 %reduce-scatter.2.cloned.1.call-done = f32[8,4,8,2,256]{4,2,3,1,0:T(8,128)} async-done(((f32[16,4,8,2,256]{4,2,3,1,0:T(8,128)}), f32[8,4,8,2,256]{4,2,3,1,0:T(8,128)}) %reduce-scatter.2.cloned.1.call-update) | async-done | bytes 524304 | tf_op jit(solution)/shard_map/reduce_scatter | solution.py:79
  142.0 1.9 %copy.46 = f32[8,4,8,2,256]{4,2,0,1,3:T(8,128)} copy(f32[8,4,8,2,256]{4,2,3,1,0:T(8,128)} %reduce-scatter.2.cloned.1.call-done) | data formatting | bytes 1048576 | tf_op jit(solution)/shard_map/reduce_scatter | solution.py:79
  (13 shorter events, 0.0 us)
Async XLA Ops:
  6.5 55.7 %copy-start.8 = (s32[64,1]{0,1:T(1,128)S(1)}, s32[64,1]{0,1:T(1,128)}, u32[]{:S(2)}) copy-start(s32[64,1]{0,1:T(1,128)} %param.5) | copy-start | bytes 772
  6.5 135.4 %reduce-scatter.2.cloned.1.call-start = ((), (), s32[]{:S(2)}) async-start(), calls=%async_computation.2 | async-start | bytes 1572864 | tf_op jit(solution)/shard_map/reduce_scatter | solution.py:79
  52.2 0.8 copy-start.4
  70.3 2.4 %copy-start.5 = (bf16[32,2,4096]{2,1,0:T(2,128)(2,1)S(1)}, bf16[32,2,4096]{2,1,0:T(2,128)(2,1)}, u32[]{:S(2)}) copy-start(bf16[32,2,4096]{2,1,0:T(2,128)(2,1)} %copy-done.4) | copy-start | bytes 1572868
  78.9 2.3 %copy-start.1 = (f32[112,8192]{1,0:T(8,128)S(1)}, f32[112,8192]{1,0:T(8,128)}, u32[]{:S(2)}) copy-start(f32[112,8192]{1,0:T(8,128)} %slice.103) | copy-start | bytes 11010052
  78.9 2.4 %copy-start.6 = (f32[16,8192]{1,0:T(8,128)S(1)}, f32[16,8192]{1,0:T(8,128)}, u32[]{:S(2)}) copy-start(f32[16,8192]{1,0:T(8,128)} %slice.102) | copy-start | bytes 1572868
  81.3 2.1 %copy-start = (f32[120,8192]{1,0:T(8,128)S(1)}, f32[120,8192]{1,0:T(8,128)}, u32[]{:S(2)}) copy-start(f32[120,8192]{1,0:T(8,128)} %slice.99) | copy-start | bytes 11796484
  81.3 2.1 %copy-start.7 = (f32[8,8192]{1,0:T(8,128)S(1)}, f32[8,8192]{1,0:T(8,128)}, u32[]{:S(2)}) copy-start(f32[8,8192]{1,0:T(8,128)} %slice.98) | copy-start | bytes 786436
  83.4 1.6 %copy-start.2 = (f32[16,8,4,1024]{3,1,2,0:T(8,128)S(1)}, f32[16,8,4,1024]{3,1,2,0:T(8,128)}, u32[]{:S(2)}) copy-start(f32[16,8,4,1024]{3,1,2,0:T(8,128)} %get-tuple-element.27) | copy-start | bytes 6291460
  83.4 2.2 %copy-start.3 = (f32[16,8,4,1024]{3,1,2,0:T(8,128)S(1)}, f32[16,8,4,1024]{3,1,2,0:T(8,128)}, u32[]{:S(2)}) copy-start(f32[16,8,4,1024]{3,1,2,0:T(8,128)} %get-tuple-element.28) | copy-start | bytes 6291460
Sparse Core Ops, SparseCore 0:
  134.9 7.0 reduce-scatter.1
where the time goes:
time: 151 us
  blocking collectives  66.2 us (44%)
  local copies, waits for them, and re-layouts  35.1 us (23%)
  other arithmetic  24.5 us (16%)
  between operations  13.6 us (9%)
  waiting for transfers between devices  7.22 us (5%)
  matrix products  4.13 us (3%)
    all_gather x1, blocking collectives, per_device(): all_sources = lax.all_gather(sources, 'blk', axis=0, tiled=True)  45.7 us
    all_to_all x1, blocking collectives, per_device(): lax.all_to_all(partial, 'blk', split_axis=0, concat_axis=0, tiled=True)  18.1 us
    reduce_sum x1, other arithmetic, per_device(): even = jnp.sum(real_t * real_s + imag_t * imag_s, axis=3)  7.3 us
    reduce_scatter x1, waiting for transfers between devices, per_device(): lax.psum_scatter(arrived.astype(jnp.float32), 'band', scatter_dimension=0...  7.2 us
    convert_element_type x1, local copies, waits for them, and re-layouts, per_device(): cross = jnp.stack(cross, axis=1).astype(jnp.bfloat16)  7.2 us
    slice x6, local copies, waits for them, and re-layouts, per_device(): visiting = jnp.roll(placed, offset, axis=0)  6.99 us
    another operation x1, local copies, waits for them, and re-layouts, per_device(): cross = jnp.stack(cross, axis=1).astype(jnp.bfloat16)  6.3 us
    unnamed x19, local copies, waits for them, and re-layouts  5.42 us
  transfers between devices with their start and end apart: 1, of which 1 were waited for; matrix products, arithmetic and copies ran while one was open for 0% of the time, Pallas kernels for 0%

commit v1 on v0

--- a/solution.py
+++ b/solution.py
@@ -9,6 +9,18 @@
 DEC = 8
 PERIOD = BINS // DEC
 EPS = 1e-06
+
+
+def exchange_directly(x, axis, split, join):
+    ways, here = (lax.axis_size(axis), lax.axis_index(axis))
+    width = x.shape[split] // ways
+    turned = jnp.roll(x, -here * width, axis=split)
+    got = [lax.slice_in_dim(turned, 0, width, axis=split)]
+    for far in range(1, ways):
+        sent = lax.slice_in_dim(turned, far * width, (far + 1) * width, axis=split)
+        got.append(lax.ppermute(sent, axis, [(d, (d + far) % ways) for d in range(ways)]))
+    line = jnp.concatenate(got[::-1], axis=join)
+    return jnp.roll(line, (here + 1) * got[0].shape[join], axis=join)
 
 
 def per_device(traces, sources, owner):
@@ -75,7 +87,7 @@
     partial = jnp.dot(cross.reshape(rows, 2 * PERIOD), table, preferred_element_type=jnp.float32)
     partial = (partial * norm_scale).astype(jnp.bfloat16)
     partial = partial.reshape(blocks, offsets, capacity, source_count, lags_out)
-    arrived = lax.all_to_all(partial, "blk", split_axis=0, concat_axis=0, tiled=True)
+    arrived = exchange_directly(partial, "blk", 0, 0)
     summed = lax.psum_scatter(arrived.astype(jnp.float32), "band", scatter_dimension=0, tiled=True)
     half = summed.shape[0]
     return jnp.transpose(summed, (3, 1, 0, 2, 4)).reshape(

time: 151 us -> 164 us (1.086)
  starting transfers between devices: 0.01 us -> 20.7 us
  blocking collectives: 66.2 us -> 48.1 us
  waiting for transfers between devices: 7.22 us -> 13.6 us
  local copies, waits for them, and re-layouts: 35.1 us -> 38 us
    ppermute x0 -> x15, starting transfers between devices: none -> 20.7 us  [exchange_directly(): lax.ppermute(sent, axis, [(d, (d + far) % ways) for d in range(ways)])]
    all_to_all x1 -> x0, blocking collectives: 18.1 us -> none  [per_device(): lax.all_to_all(partial, 'blk', split_axis=0, concat_axis=0, tiled=True)]
    ppermute x0 -> x15, waiting for transfers between devices: none -> 6.59 us  [exchange_directly(): lax.ppermute(sent, axis, [(d, (d + far) % ways) for d in range(ways)])]
    mul x2, local copies, waits for them, and re-layouts: 3.67 us -> 6.21 us  [per_device(): even = jnp.sum(real_t * real_s + imag_t * imag_s, axis=3)]
    unnamed x19 -> x36, local copies, waits for them, and re-layouts: 5.42 us -> 5.48 us
  transfers between devices with their start and end apart: 1 -> 16, of which waited for: 1 -> 6; matrix products, arithmetic and copies ran while one was open for 0% -> 0% of each run, Pallas kernels for 0% -> 0%
where the time goes in v1:
time: 164 us; the launch traced here: 163 us
  blocking collectives  48.1 us (29%)
  local copies, waits for them, and re-layouts  38 us (23%)
  other arithmetic  24.8 us (15%)
  starting transfers between devices  20.7 us (13%)
  between operations  13.7 us (8%)
  waiting for transfers between devices  13.6 us (8%)
  matrix products  4.13 us (3%)
    all_gather x1, blocking collectives, per_device(): all_sources = lax.all_gather(sources, 'blk', axis=0, tiled=True)  45.7 us
    ppermute x15, starting transfers between devices, exchange_directly(): lax.ppermute(sent, axis, [(d, (d + far) % ways) for d in range(ways)])  20.7 us
    reduce_sum x1, other arithmetic, per_device(): even = jnp.sum(real_t * real_s + imag_t * imag_s, axis=3)  7.3 us
    slice x6, local copies, waits for them, and re-layouts, per_device(): visiting = jnp.roll(placed, offset, axis=0)  7.26 us
    convert_element_type x1, local copies, waits for them, and re-layouts, per_device(): cross = jnp.stack(cross, axis=1).astype(jnp.bfloat16)  7.2 us
    reduce_scatter x1, waiting for transfers between devices, per_device(): lax.psum_scatter(arrived.astype(jnp.float32), 'band', scatter_dimension=0...  6.95 us
    ppermute x15, waiting for transfers between devices, exchange_directly(): lax.ppermute(sent, axis, [(d, (d + far) % ways) for d in range(ways)])  6.59 us
    another operation x1, local copies, waits for them, and re-layouts, per_device(): cross = jnp.stack(cross, axis=1).astype(jnp.bfloat16)  6.3 us
  transfers between devices with their start and end apart: 16, of which 6 were waited for; matrix products, arithmetic and copies ran while one was open for 0% of the time, Pallas kernels for 0%

profile of v1, /device:TPU:0, one launch (start us, length us, event | category | flops | bytes accessed | tf_op | source)
XLA Modules:
  0.0 163.0 jit_solution(17361109270526813846)
XLA Ops:
  6.5 45.7 %all_gather.3 = bf16[32,2,4096]{2,1,0:T(2,128)(2,1)S(1)} all-gather(bf16[2,2,4096]{2,1,0:T(2,128)(2,1)} %param.6), channel_id=1, replica_groups=mesh['blk'=16,'band'=2] {'blk'}, dimensions={0}, use_global_device_ids=true | all-gather | bytes 557056 | tf_op jit(solution)/shard_map/all_gather | solution.py:35
  52.2 0.8 copy-done.5
  53.0 0.8 fusion.12
  53.8 2.8 %fusion = f32[64]{0:T(128)S(1)} fusion(bf16[64,2,4096]{2,1,0:T(2,128)(2,1)} %param.5), kind=kLoop, calls=%fused_computation.17 | loop fusion | flops 1572800 | bytes 1048832 | tf_op jit(solution)/shard_map/reduce_sum | solution.py:40
  56.6 2.5 %all-reduce = (f32[32]{0:T(128)S(1)}, f32[64]{0:T(128)S(1)}) all-reduce(f32[32]{0:T(128)S(1)} %fusion.12, f32[64]{0:T(128)S(1)} %fusion), channel_id=1, replica_groups=mesh['blk'=16,'band'=2] {'band'}, use_global_device_ids=true, to_apply=%region_5.6 | all-reduce | flops 96 | bytes 768 | tf_op jit(solution)/shard_map/psum | solution.py:38
  59.1 2.5 %fusion.1 = bf16[64,2,4096]{2,1,0:T(2,128)(2,1)S(1)} fusion(bf16[64,2,4096]{2,1,0:T(2,128)(2,1)} %param.5, f32[64]{0:T(128)S(1)} %add_rsqrt_fusion.1), kind=kLoop, calls=%fused_computation.18 | loop fusion | flops 1572864 | bytes 2097408 | tf_op jit(solution)/shard_map/convert_element_type | solution.py:47
  61.6 0.6 copy.47
  62.6 0.7 fusion.27
  63.3 0.2 slice.171
  63.6 1.2 slice.170
  64.7 2.2 %slice.167 = f32[112,8192]{1,0:T(8,128)} slice(f32[128,8192]{1,0:T(8,128)S(1)} %fusion.27), slice={[0:112], [0:8192]} | slice | bytes 7340032 | tf_op jit(solution)/shard_map/jit(_roll_static)/slice | solution.py:79
  66.9 0.8 slice.166
  67.7 2.2 %slice.163 = f32[120,8192]{1,0:T(8,128)} slice(f32[128,8192]{1,0:T(8,128)S(1)} %fusion.27), slice={[0:120], [0:8192]} | slice | bytes 7864320 | tf_op jit(solution)/shard_map/jit(_roll_static)/slice | solution.py:79
  69.9 0.7 slice.162
  70.6 4.9 %slice_bitcast_fusion.1 = (f32[16,8,4,1024]{3,1,2,0:T(8,128)}, f32[16,8,4,1024]{3,1,2,0:T(8,128)}) fusion(f32[16,8,2,4,1024]{4,1,3,2,0:T(8,128)} %bitcast.46), kind=kLoop, calls=%fused_computation.32 | loop fusion | bytes 8388608 | tf_op jit(solution)/shard_map/mul | solution.py:82
  75.5 1.5 fusion.23
  77.0 3.3 %reshape.51 = f32[16,2,2,4,1024]{4,3,2,1,0:T(4,128)} reshape(f32[32,2,4096]{2,1,0:T(2,128)} %fusion.23) | data formatting | bytes 2097152 | tf_op jit(solution)/shard_map/reshape | solution.py:54
  80.4 1.3 slice_bitcast_fusion.3
  81.7 1.6 fusion.3
  83.3 0.6 copy-done.2
  84.1 0.5 fusion.5
  84.6 1.6 copy-done.1
  86.2 0.5 fusion.7
  86.7 1.1 copy-done.3
  87.8 0.6 copy-done.4
  88.4 7.3 %add_reduce_fusion.3 = (bf16[16,8,2,1024]{3,1,2,0:T(8,128)(2,1)S(1)}, bf16[16,8,2,1024]{3,1,2,0:T(8,128)(2,1)S(1)}, bf16[16,8,2,1024]{3,1,2,0:T(8,128)(2,1)S(1)}...) fusion(f32[16,2,4,1024]{3,2,1,0:T(4,128)S(1)} %get-tuple-elemen, ...), kind=kLoop, calls=%fused_computation.14 | loop fusion | flops 31457280 | bytes 22020096 | tf_op jit(solution)/shard_map/reduce_sum | solution.py:82
  96.1 0.6 pad_maximum_fusion
  96.7 6.3 %copy.43 = bf16[16,4,8,2,2048]{4,3,2,1,0:T(2,128)(2,1)} copy(bf16[16,4,8,2,2048]{4,2,3,0,1:T(8,128)(2,1)S(1)} %pad_maximum_fusion) | data formatting | bytes 8388608 | tf_op jit(solution)/shard_map/stack | solution.py:85
  103.0 7.2 %convert_element_type.39 = bf16[1024,2048]{1,0:T(8,128)(2,1)} reshape(bf16[16,4,8,2,2048]{4,3,2,1,0:T(2,128)(2,1)} %copy.43) | data formatting | bytes 8388608 | tf_op jit(solution)/shard_map/convert_element_type | solution.py:85
  110.2 4.4 %cosine_convert_fusion = (bf16[1024,256]{1,0:T(8,128)(2,1)S(1)}, bf16[1024,256]{1,0:T(8,128)(2,1)S(1)}) fusion(s32[256]{0:T(256)S(1)} %add_multiply_fusion), kind=kLoop, calls=%fused_computation.57 | loop fusion | flops 4194304 | bytes 1049600 | tf_op jit(solution)/shard_map/convert.1
  114.6 3.4 %fusion.11 = bf16[1024,256]{1,0:T(8,128)(2,1)S(1)} fusion(bf16[1024,2048]{1,0:T(8,128)(2,1)} %convert_element_type.39, bf16[1024,256]{1,0:T(8,128)(2,1)S(1)} %get-tuple-element.48, bf16[1024,256]{1,0:T(8,128)(2,1)S(1)} %get-tuple-element.47), kind=kOutput, calls=%fused_computation.39 | convolution fusion | flops 1076363264 | bytes 5767168 | tf_op jit(solution)/shard_map/dot_general | solution.py:87
  118.4 0.2 fusion.26
  118.9 3.5 %collective-permute-start.4 = (bf16[1,4,8,2,256]{4,2,3,1,0:T(8,128)(2,1)S(1)}, bf16[1,4,8,2,256]{4,2,3,1,0:T(8,128)(2,1)S(1)}, u32[]{:S(2)}, u32[]{:S(2)}) collective-permute-start(bf16[1,4,8,2,256]{4,2,3,1,0:T(8,128)(2,1)S(1)} %get-tuple-element.42), channel_id=1, source_target_pairs={{0,22},{2,24},{4,26},{6,28},{8,30},{10,0},{12,2},{14,4},{16,6},{18... | collective-permute-start | bytes 98312 | tf_op jit(solution)/shard_map/ppermute | solution.py:21
  122.3 0.2 collective-permute-done
  122.6 2.9 %collective-permute-start.5 = (bf16[1,4,8,2,256]{4,2,3,1,0:T(8,128)(2,1)S(1)}, bf16[1,4,8,2,256]{4,2,3,1,0:T(8,128)(2,1)S(1)}, u32[]{:S(2)}, u32[]{:S(2)}) collective-permute-start(bf16[1,4,8,2,256]{4,2,3,1,0:T(8,128)(2,1)S(1)} %get-tuple-element.41), channel_id=1, source_target_pairs={{0,20},{2,22},{4,24},{6,26},{8,28},{10,30},{12,0},{14,2},{16,4},{1... | collective-permute-start | bytes 98312 | tf_op jit(solution)/shard_map/ppermute | solution.py:21
  125.5 3.4 %collective-permute-start.7 = (bf16[1,4,8,2,256]{4,2,3,1,0:T(8,128)(2,1)S(1)}, bf16[1,4,8,2,256]{4,2,3,1,0:T(8,128)(2,1)S(1)}, u32[]{:S(2)}, u32[]{:S(2)}) collective-permute-start(bf16[1,4,8,2,256]{4,2,3,1,0:T(8,128)(2,1)S(1)} %get-tuple-element.39), channel_id=1, source_target_pairs={{0,16},{2,18},{4,20},{6,22},{8,24},{10,26},{12,28},{14,30},{16,0},... | collective-permute-start | bytes 98312 | tf_op jit(solution)/shard_map/ppermute | solution.py:21
  128.9 0.5 collective-permute-start.8
  129.4 2.9 %collective-permute-start.9 = (bf16[1,4,8,2,256]{4,2,3,1,0:T(8,128)(2,1)S(1)}, bf16[1,4,8,2,256]{4,2,3,1,0:T(8,128)(2,1)S(1)}, u32[]{:S(2)}, u32[]{:S(2)}) collective-permute-start(bf16[1,4,8,2,256]{4,2,3,1,0:T(8,128)(2,1)S(1)} %get-tuple-element.37), channel_id=1, source_target_pairs={{0,12},{2,14},{4,16},{6,18},{8,20},{10,22},{12,24},{14,26},{16,28}... | collective-permute-start | bytes 98312 | tf_op jit(solution)/shard_map/ppermute | solution.py:21
  132.3 1.9 %collective-permute-start.10 = (bf16[1,4,8,2,256]{4,2,3,1,0:T(8,128)(2,1)S(1)}, bf16[1,4,8,2,256]{4,2,3,1,0:T(8,128)(2,1)S(1)}, u32[]{:S(2)}, u32[]{:S(2)}) collective-permute-start(bf16[1,4,8,2,256]{4,2,3,1,0:T(8,128)(2,1)S(1)} %get-tuple-element.36), channel_id=1, source_target_pairs={{0,10},{2,12},{4,14},{6,16},{8,18},{10,20},{12,22},{14,24},{16,26}... | collective-permute-start | bytes 98312 | tf_op jit(solution)/shard_map/ppermute | solution.py:21
  134.3 1.0 collective-permute-start.11
  135.2 3.3 %collective-permute-start.12 = (bf16[1,4,8,2,256]{4,2,3,1,0:T(8,128)(2,1)S(1)}, bf16[1,4,8,2,256]{4,2,3,1,0:T(8,128)(2,1)S(1)}, u32[]{:S(2)}, u32[]{:S(2)}) collective-permute-start(bf16[1,4,8,2,256]{4,2,3,1,0:T(8,128)(2,1)S(1)} %get-tuple-element.34), channel_id=1, source_target_pairs={{0,6},{2,8},{4,10},{6,12},{8,14},{10,16},{12,18},{14,20},{16,22},{... | collective-permute-start | bytes 98312 | tf_op jit(solution)/shard_map/ppermute | solution.py:21
  138.5 1.2 collective-permute-start.14
  140.0 3.1 %collective-permute-done.12 = bf16[1,4,8,2,256]{4,2,3,1,0:T(8,128)(2,1)S(1)} collective-permute-done((bf16[1,4,8,2,256]{4,2,3,1,0:T(8,128)(2,1)S(1)}, bf16[1,4,8,2,256]{4,2,3,1,0:T(8,128)(2,1)S(1)}, u32[]{:S(2)}, u32[]{:S(2)}) %collective-permute-start.12) | collective-permute-done | bytes 32800 | tf_op jit(solution)/shard_map/ppermute | solution.py:21
  143.1 2.0 %collective-permute-done.13 = bf16[1,4,8,2,256]{4,2,3,1,0:T(8,128)(2,1)S(1)} collective-permute-done((bf16[1,4,8,2,256]{4,2,3,1,0:T(8,128)(2,1)S(1)}, bf16[1,4,8,2,256]{4,2,3,1,0:T(8,128)(2,1)S(1)}, u32[]{:S(2)}, u32[]{:S(2)}) %collective-permute-start.13) | collective-permute-done | bytes 32800 | tf_op jit(solution)/shard_map/ppermute | solution.py:21
  145.1 1.0 collective-permute-done.14
  146.1 1.2 fusion.25
  147.4 7.0 %reduce-scatter.2.cloned.1.call-done = f32[8,4,8,2,256]{4,2,3,1,0:T(8,128)} async-done(((f32[16,4,8,2,256]{4,2,3,1,0:T(8,128)}), f32[8,4,8,2,256]{4,2,3,1,0:T(8,128)}) %reduce-scatter.2.cloned.1.call-update) | async-done | bytes 524304 | tf_op jit(solution)/shard_map/reduce_scatter | solution.py:91
  154.3 1.9 %copy.49 = f32[8,4,8,2,256]{4,2,0,1,3:T(8,128)} copy(f32[8,4,8,2,256]{4,2,3,1,0:T(8,128)} %reduce-scatter.2.cloned.1.call-done) | data formatting | bytes 1048576 | tf_op jit(solution)/shard_map/reduce_scatter | solution.py:91
  (62 shorter events, 1.8 us)
Async XLA Ops:
  6.5 55.7 %copy-start.9 = (s32[64,1]{0,1:T(1,128)S(1)}, s32[64,1]{0,1:T(1,128)}, u32[]{:S(2)}) copy-start(s32[64,1]{0,1:T(1,128)} %param.7) | copy-start | bytes 772
  6.5 147.8 %reduce-scatter.2.cloned.1.call-start = ((), (), s32[]{:S(2)}) async-start(), calls=%async_computation.1 | async-start | bytes 1572864 | tf_op jit(solution)/shard_map/reduce_scatter | solution.py:91
  52.2 0.8 copy-start.5
  63.3 6.6 %copy-start = (f32[128,8192]{1,0:T(8,128)}, f32[128,8192]{1,0:T(8,128)S(1)}, u32[]{:S(2)}) copy-start(f32[128,8192]{1,0:T(8,128)S(1)} %fusion.27) | copy-start | bytes 12582916
  70.6 4.9 %copy-start.6 = (bf16[32,2,4096]{2,1,0:T(2,128)(2,1)S(1)}, bf16[32,2,4096]{2,1,0:T(2,128)(2,1)}, u32[]{:S(2)}) copy-start(bf16[32,2,4096]{2,1,0:T(2,128)(2,1)} %copy-done.5) | copy-start | bytes 1572868
  81.7 2.3 %copy-start.2 = (f32[112,8192]{1,0:T(8,128)S(1)}, f32[112,8192]{1,0:T(8,128)}, u32[]{:S(2)}) copy-start(f32[112,8192]{1,0:T(8,128)} %slice.167) | copy-start | bytes 11010052
  81.7 2.4 %copy-start.7 = (f32[16,8192]{1,0:T(8,128)S(1)}, f32[16,8192]{1,0:T(8,128)}, u32[]{:S(2)}) copy-start(f32[16,8192]{1,0:T(8,128)} %slice.166) | copy-start | bytes 1572868
  84.1 2.1 %copy-start.1 = (f32[120,8192]{1,0:T(8,128)S(1)}, f32[120,8192]{1,0:T(8,128)}, u32[]{:S(2)}) copy-start(f32[120,8192]{1,0:T(8,128)} %slice.163) | copy-start | bytes 11796484
  84.1 2.1 %copy-start.8 = (f32[8,8192]{1,0:T(8,128)S(1)}, f32[8,8192]{1,0:T(8,128)}, u32[]{:S(2)}) copy-start(f32[8,8192]{1,0:T(8,128)} %slice.162) | copy-start | bytes 786436
  86.2 1.6 copy-start.3
  86.2 2.2 %copy-start.4 = (f32[16,8,4,1024]{3,1,2,0:T(8,128)S(1)}, f32[16,8,4,1024]{3,1,2,0:T(8,128)}, u32[]{:S(2)}) copy-start(f32[16,8,4,1024]{3,1,2,0:T(8,128)} %get-tuple-element.29) | copy-start | bytes 6291460
  118.6 4.0 %collective-permute-start = (bf16[1,4,8,2,256]{4,2,3,1,0:T(8,128)(2,1)S(1)}, bf16[1,4,8,2,256]{4,2,3,1,0:T(8,128)(2,1)S(1)}, u32[]{:S(2)}, u32[]{:S(2)}) collective-permute-start(bf16[1,4,8,2,256]{4,2,3,1,0:T(8,128)(2,1)S(1)} %get-tuple-element.46), channel_id=1, source_target_pairs={{0,30},{2,0},{4,2},{6,4},{8,6},{10,8},{12,10},{14,12},{16,14},{18,... | collective-permute-start | bytes 98312 | tf_op jit(solution)/shard_map/ppermute | solution.py:21
  118.7 6.8 %collective-permute-start.1 = (bf16[1,4,8,2,256]{4,2,3,1,0:T(8,128)(2,1)S(1)}, bf16[1,4,8,2,256]{4,2,3,1,0:T(8,128)(2,1)S(1)}, u32[]{:S(2)}, u32[]{:S(2)}) collective-permute-start(bf16[1,4,8,2,256]{4,2,3,1,0:T(8,128)(2,1)S(1)} %get-tuple-element.45), channel_id=1, source_target_pairs={{0,28},{2,30},{4,0},{6,2},{8,4},{10,6},{12,8},{14,10},{16,12},{18,... | collective-permute-start | bytes 98312 | tf_op jit(solution)/shard_map/ppermute | solution.py:21
  118.8 6.8 %collective-permute-start.2 = (bf16[1,4,8,2,256]{4,2,3,1,0:T(8,128)(2,1)S(1)}, bf16[1,4,8,2,256]{4,2,3,1,0:T(8,128)(2,1)S(1)}, u32[]{:S(2)}, u32[]{:S(2)}) collective-permute-start(bf16[1,4,8,2,256]{4,2,3,1,0:T(8,128)(2,1)S(1)} %get-tuple-element.44), channel_id=1, source_target_pairs={{0,26},{2,28},{4,30},{6,0},{8,2},{10,4},{12,6},{14,8},{16,10},{18,... | collective-permute-start | bytes 98312 | tf_op jit(solution)/shard_map/ppermute | solution.py:21
  118.8 10.1 %collective-permute-start.3 = (bf16[1,4,8,2,256]{4,2,3,1,0:T(8,128)(2,1)S(1)}, bf16[1,4,8,2,256]{4,2,3,1,0:T(8,128)(2,1)S(1)}, u32[]{:S(2)}, u32[]{:S(2)}) collective-permute-start(bf16[1,4,8,2,256]{4,2,3,1,0:T(8,128)(2,1)S(1)} %get-tuple-element.43), channel_id=1, source_target_pairs={{0,24},{2,26},{4,28},{6,30},{8,0},{10,2},{12,4},{14,6},{16,8},{18,... | collective-permute-start | bytes 98312 | tf_op jit(solution)/shard_map/ppermute | solution.py:21
  118.9 10.5 %collective-permute-start.4 = (bf16[1,4,8,2,256]{4,2,3,1,0:T(8,128)(2,1)S(1)}, bf16[1,4,8,2,256]{4,2,3,1,0:T(8,128)(2,1)S(1)}, u32[]{:S(2)}, u32[]{:S(2)}) collective-permute-start(bf16[1,4,8,2,256]{4,2,3,1,0:T(8,128)(2,1)S(1)} %get-tuple-element.42), channel_id=1, source_target_pairs={{0,22},{2,24},{4,26},{6,28},{8,30},{10,0},{12,2},{14,4},{16,6},{18... | collective-permute-start | bytes 98312 | tf_op jit(solution)/shard_map/ppermute | solution.py:21
  122.6 9.8 %collective-permute-start.5 = (bf16[1,4,8,2,256]{4,2,3,1,0:T(8,128)(2,1)S(1)}, bf16[1,4,8,2,256]{4,2,3,1,0:T(8,128)(2,1)S(1)}, u32[]{:S(2)}, u32[]{:S(2)}) collective-permute-start(bf16[1,4,8,2,256]{4,2,3,1,0:T(8,128)(2,1)S(1)} %get-tuple-element.41), channel_id=1, source_target_pairs={{0,20},{2,22},{4,24},{6,26},{8,28},{10,30},{12,0},{14,2},{16,4},{1... | collective-permute-start | bytes 98312 | tf_op jit(solution)/shard_map/ppermute | solution.py:21
  125.5 8.7 %collective-permute-start.6 = (bf16[1,4,8,2,256]{4,2,3,1,0:T(8,128)(2,1)S(1)}, bf16[1,4,8,2,256]{4,2,3,1,0:T(8,128)(2,1)S(1)}, u32[]{:S(2)}, u32[]{:S(2)}) collective-permute-start(bf16[1,4,8,2,256]{4,2,3,1,0:T(8,128)(2,1)S(1)} %get-tuple-element.40), channel_id=1, source_target_pairs={{0,18},{2,20},{4,22},{6,24},{8,26},{10,28},{12,30},{14,0},{16,2},{... | collective-permute-start | bytes 98312 | tf_op jit(solution)/shard_map/ppermute | solution.py:21
  125.5 9.7 %collective-permute-start.7 = (bf16[1,4,8,2,256]{4,2,3,1,0:T(8,128)(2,1)S(1)}, bf16[1,4,8,2,256]{4,2,3,1,0:T(8,128)(2,1)S(1)}, u32[]{:S(2)}, u32[]{:S(2)}) collective-permute-start(bf16[1,4,8,2,256]{4,2,3,1,0:T(8,128)(2,1)S(1)} %get-tuple-element.39), channel_id=1, source_target_pairs={{0,16},{2,18},{4,20},{6,22},{8,24},{10,26},{12,28},{14,30},{16,0},... | collective-permute-start | bytes 98312 | tf_op jit(solution)/shard_map/ppermute | solution.py:21
  128.9 9.6 %collective-permute-start.8 = (bf16[1,4,8,2,256]{4,2,3,1,0:T(8,128)(2,1)S(1)}, bf16[1,4,8,2,256]{4,2,3,1,0:T(8,128)(2,1)S(1)}, u32[]{:S(2)}, u32[]{:S(2)}) collective-permute-start(bf16[1,4,8,2,256]{4,2,3,1,0:T(8,128)(2,1)S(1)} %get-tuple-element.38), channel_id=1, source_target_pairs={{0,14},{2,16},{4,18},{6,20},{8,22},{10,24},{12,26},{14,28},{16,30}... | collective-permute-start | bytes 98312 | tf_op jit(solution)/shard_map/ppermute | solution.py:21
  129.4 9.1 %collective-permute-start.9 = (bf16[1,4,8,2,256]{4,2,3,1,0:T(8,128)(2,1)S(1)}, bf16[1,4,8,2,256]{4,2,3,1,0:T(8,128)(2,1)S(1)}, u32[]{:S(2)}, u32[]{:S(2)}) collective-permute-start(bf16[1,4,8,2,256]{4,2,3,1,0:T(8,128)(2,1)S(1)} %get-tuple-element.37), channel_id=1, source_target_pairs={{0,12},{2,14},{4,16},{6,18},{8,20},{10,22},{12,24},{14,26},{16,28}... | collective-permute-start | bytes 98312 | tf_op jit(solution)/shard_map/ppermute | solution.py:21
  132.3 7.4 %collective-permute-start.10 = (bf16[1,4,8,2,256]{4,2,3,1,0:T(8,128)(2,1)S(1)}, bf16[1,4,8,2,256]{4,2,3,1,0:T(8,128)(2,1)S(1)}, u32[]{:S(2)}, u32[]{:S(2)}) collective-permute-start(bf16[1,4,8,2,256]{4,2,3,1,0:T(8,128)(2,1)S(1)} %get-tuple-element.36), channel_id=1, source_target_pairs={{0,10},{2,12},{4,14},{6,16},{8,18},{10,20},{12,22},{14,24},{16,26}... | collective-permute-start | bytes 98312 | tf_op jit(solution)/shard_map/ppermute | solution.py:21
  134.3 5.7 %collective-permute-start.11 = (bf16[1,4,8,2,256]{4,2,3,1,0:T(8,128)(2,1)S(1)}, bf16[1,4,8,2,256]{4,2,3,1,0:T(8,128)(2,1)S(1)}, u32[]{:S(2)}, u32[]{:S(2)}) collective-permute-start(bf16[1,4,8,2,256]{4,2,3,1,0:T(8,128)(2,1)S(1)} %get-tuple-element.35), channel_id=1, source_target_pairs={{0,8},{2,10},{4,12},{6,14},{8,16},{10,18},{12,20},{14,22},{16,24},... | collective-permute-start | bytes 98312 | tf_op jit(solution)/shard_map/ppermute | solution.py:21
  135.2 7.8 %collective-permute-start.12 = (bf16[1,4,8,2,256]{4,2,3,1,0:T(8,128)(2,1)S(1)}, bf16[1,4,8,2,256]{4,2,3,1,0:T(8,128)(2,1)S(1)}, u32[]{:S(2)}, u32[]{:S(2)}) collective-permute-start(bf16[1,4,8,2,256]{4,2,3,1,0:T(8,128)(2,1)S(1)} %get-tuple-element.34), channel_id=1, source_target_pairs={{0,6},{2,8},{4,10},{6,12},{8,14},{10,16},{12,18},{14,20},{16,22},{... | collective-permute-start | bytes 98312 | tf_op jit(solution)/shard_map/ppermute | solution.py:21
  138.5 6.6 %collective-permute-start.13 = (bf16[1,4,8,2,256]{4,2,3,1,0:T(8,128)(2,1)S(1)}, bf16[1,4,8,2,256]{4,2,3,1,0:T(8,128)(2,1)S(1)}, u32[]{:S(2)}, u32[]{:S(2)}) collective-permute-start(bf16[1,4,8,2,256]{4,2,3,1,0:T(8,128)(2,1)S(1)} %get-tuple-element.33), channel_id=1, source_target_pairs={{0,4},{2,6},{4,8},{6,10},{8,12},{10,14},{12,16},{14,18},{16,20},{1... | collective-permute-start | bytes 98312 | tf_op jit(solution)/shard_map/ppermute | solution.py:21
  138.5 7.6 %collective-permute-start.14 = (bf16[1,4,8,2,256]{4,2,3,1,0:T(8,128)(2,1)S(1)}, bf16[1,4,8,2,256]{4,2,3,1,0:T(8,128)(2,1)S(1)}, u32[]{:S(2)}, u32[]{:S(2)}) collective-permute-start(bf16[1,4,8,2,256]{4,2,3,1,0:T(8,128)(2,1)S(1)} %get-tuple-element.32), channel_id=1, source_target_pairs={{0,2},{2,4},{4,6},{6,8},{8,10},{10,12},{12,14},{14,16},{16,18},{18... | collective-permute-start | bytes 98312 | tf_op jit(solution)/shard_map/ppermute | solution.py:21
Sparse Core Ops, SparseCore 0:
  147.5 6.7 reduce-scatter.1
